TPU v7x, 256 devices: a whole 4x4x8 slice. The times are simulated.
256 devices in a mesh: path: 64 (over z, x, core), rep: 4 (over y).
Axes of the slice: x: 4, y: 4, z: 8, core: 2. Of those that a mesh axis runs over, the one named last changes fastest.
Arguments:
- start_state: float32 [32, 65536], P(None, 'path'), may hold values from -1.8 to 1.8
- increments: float32 [2, 32, 65536], P(None, None, 'path'), may hold values from -6 to 6
- vol_factor: float32 [32, 32], replicated, may hold values from -0.3 to 0.3
- quad_dirs: float32 [223, 32], replicated, may hold values from -1.5 to 1.5
- bundle_ids: int32 [2, 65536, 1], P(None, 'path'), may hold values from 0 to 255; in each aligned block of 1024 rows (0 to 1023, 1024 to 2047, ..., all dimensions but the last counted through in order) at most 8 rows name the same one
- bundle_slot: int32 [256], replicated, may hold values from 0 to 255, each once
Outputs:
- values: float32 [2, 65536], P(None, 'path')
- coefficients: float32 [2, 256, 256], P(None, 'path', 'rep')
Inputs may be any that keep to these rules, and one draw needn't show every extreme that they name: `bundle_ids`: at each date, no bundle id appears more than 8 times among the paths of one device; in every draw some device holds exactly 8 paths of one bundle. A permutation: bundle b sits at slot bundle_slot[b], and slot s belongs to the owner s // 4 along path.
All inputs are finite; a program needn't handle non-finite values.
Results may differ from a plain program's by a relative error of at most 0.0003.
Values sent between devices are 32-bit elements; how exact they have to be, the bound alone decides.
No kernel may reach another device: no remote copies, remote signals or barrier semaphores. Data moves between devices by JAX's collectives and lax.ppermute only.
A program may use at most 64 MiB of HBM per device.

v0:
```python
import jax
import jax.numpy as jnp
from jax import lax
from jax.sharding import PartitionSpec as P

BASIS = 256
RIDGE_TERM = 32.0
DISCOUNT = 0.97
NOTIONAL = 10.0
HIGHEST = lax.Precision.HIGHEST


def basis_features(states, quad_dirs):
    projected = jnp.dot(quad_dirs, states, precision=HIGHEST, preferred_element_type=jnp.float32)
    constant = jnp.ones((1, states.shape[1]), jnp.float32)
    return jnp.concatenate([constant, states, projected * projected], axis=0)


def moment_features(states, quad_dirs, offsets):
    projected = jnp.dot(quad_dirs, states, precision=HIGHEST, preferred_element_type=jnp.float32)
    constant = jnp.ones((1, states.shape[1]), jnp.float32)
    return jnp.concatenate([constant, states, projected * projected + offsets[:, None]], axis=0)


def exercise_value(states):
    return NOTIONAL * jnp.maximum(jnp.mean(jnp.exp(states), axis=0) - 1.0, 0.0)


def backward_period(bundle_of, state_now, state_next, value_next, bundle_slot, quad_dirs, offsets):
    path_count = state_now.shape[1]
    bundles = bundle_slot.shape[0]
    owners = lax.axis_size("path")
    per_owner = bundles // owners
    capacity = max(2, 2 * path_count // bundles)
    column_count = BASIS // lax.axis_size("rep")
    rep_index = lax.axis_index("rep")
    share_count = 1
    share_slots = -(-capacity // share_count)
    padded_capacity = share_slots * share_count
    owner_block = per_owner * share_slots
    slot_of = jnp.take(bundle_slot, bundle_of)
    ranking = jnp.argsort(slot_of, stable=True)
    ordered = jnp.take(slot_of, ranking)
    group_start = jnp.searchsorted(ordered, ordered, side="left")
    rank_within = jnp.arange(path_count, dtype=jnp.int32) - group_start
    position = ordered * padded_capacity + rank_within
    regress_rows = jnp.concatenate(
        [basis_features(state_next, quad_dirs), value_next[None, :]], axis=0
    )
    row_count = regress_rows.shape[0]
    outgoing = jnp.zeros((row_count, bundles * padded_capacity), jnp.float32)
    outgoing = outgoing.at[:, position].set(jnp.take(regress_rows, ranking, axis=1))
    outgoing = outgoing.reshape(row_count, bundles, share_slots, share_count)
    outgoing = outgoing.reshape(row_count, owners, owner_block)
    arrived = lax.all_to_all(outgoing, "path", split_axis=1, concat_axis=1, tiled=True)
    arrived = arrived.reshape(row_count, owners * owner_block)
    features = arrived[:BASIS]
    target = arrived[BASIS]
    features = features.reshape(BASIS, owners, per_owner, share_slots)
    target = target.reshape(owners, per_owner, share_slots)
    column_block = lax.dynamic_slice_in_dim(features, rep_index * column_count, column_count, 0)
    gram_part = jnp.einsum("ksbm,csbm->bkc", features, column_block, precision=HIGHEST)
    gram_matrix = lax.all_gather(gram_part, "rep", axis=2, tiled=True)
    right_side = jnp.einsum("ksbm,sbm->bk", features, target, precision=HIGHEST)
    gram_matrix = gram_matrix + RIDGE_TERM * jnp.eye(BASIS, dtype=jnp.float32)
    factor = jnp.linalg.cholesky(gram_matrix)
    halfway = lax.linalg.triangular_solve(
        factor, right_side[:, :, None], left_side=True, lower=True
    )
    weights = lax.linalg.triangular_solve(
        factor, halfway, left_side=True, lower=True, transpose_a=True
    )[:, :, 0]
    weight_block = lax.dynamic_slice_in_dim(weights, rep_index * column_count, column_count, 1)
    weight_table = lax.all_gather(weight_block, "path", axis=0, tiled=True)
    picked = jnp.take(weight_table, slot_of, axis=0)
    moments = moment_features(state_now, quad_dirs, offsets)
    moment_block = lax.dynamic_slice_in_dim(moments, rep_index * column_count, column_count, 0)
    partial_terms = jnp.sum(picked.T * moment_block, axis=0)
    carried = lax.psum(partial_terms, "rep")
    value_now = jnp.maximum(exercise_value(state_now), DISCOUNT * carried)
    return (value_now, weight_block)


def body(start_state, increments, vol_factor, quad_dirs, bundle_ids, bundle_slot):
    middle = start_state + jnp.dot(
        vol_factor, increments[0], precision=HIGHEST, preferred_element_type=jnp.float32
    )
    final = middle + jnp.dot(
        vol_factor, increments[1], precision=HIGHEST, preferred_element_type=jnp.float32
    )
    mixed = jnp.dot(quad_dirs, vol_factor, precision=HIGHEST, preferred_element_type=jnp.float32)
    offsets = jnp.sum(mixed * mixed, axis=1)
    value_final = exercise_value(final)
    value_middle, weights_middle = backward_period(
        bundle_ids[0, :, 0], middle, final, value_final, bundle_slot, quad_dirs, offsets
    )
    value_start, weights_start = backward_period(
        bundle_ids[1, :, 0], start_state, middle, value_middle, bundle_slot, quad_dirs, offsets
    )
    return (jnp.stack([value_middle, value_start]), jnp.stack([weights_middle, weights_start]))


def solution(mesh):
    placed = (P(None, "path"), P(None, None, "path"), P(), P(), P(None, "path", None), P())
    return jax.shard_map(
        body,
        mesh=mesh,
        in_specs=placed,
        out_specs=(P(None, "path"), P(None, "path", "rep")),
        check_vma=False,
    )
```

profile of v0, /device:TPU:1, one launch (start us, length us, event | category | flops | bytes accessed | tf_op | source)
XLA Modules:
  0.0 985.5 jit_solution(9080812871805606301)
XLA Ops:
  7.9 6.9 gather_fusion.2
  15.4 4.4 sort.31
  19.8 4.5 gather_fusion.3
  24.3 50.7 %while.47 = (s32[]{:T(128)}, u32[1024]{0:T(1024)S(1)}, u32[1024]{0:T(1024)S(1)}, s32[1024]{0:T(1024)S(1)}, s32[]{:T(128)}, /*index=5*/s32[]{:T(128)}, s32[]{}) while((s32[]{:T(128)}, u32[1024]{0:T(1024)S(1)}, u32[1024]{0:T(1024)S(1)}, s32[1024]{0:T(1024)S(1)}, s32[]{:T(128)}, /*index=5*/s32[]{:T(128)}, s32[]{}) %tuple.133), condition=%wide.region_3.0_spmd.clone, body=%wide.region_2.5_spmd.clone.sunk | while | flops 19460 | bytes 67685 | solution.py:44
  24.4 4.5 gather_fusion
  29.0 4.5 gather_fusion
  33.6 4.5 gather_fusion
  38.2 4.5 gather_fusion
  42.8 4.5 gather_fusion
  47.4 4.5 gather_fusion
  52.0 4.5 gather_fusion
  56.7 4.5 gather_fusion
  61.3 4.5 gather_fusion
  65.9 4.5 gather_fusion
  70.5 4.5 gather_fusion
  75.1 6.9 gather_fusion.5
  82.6 4.4 sort.32
  87.5 4.5 gather_fusion.6
  92.7 50.7 %while.48 = (s32[]{:T(128)}, u32[1024]{0:T(1024)S(1)}, u32[1024]{0:T(1024)S(1)}, s32[1024]{0:T(1024)S(1)}, s32[]{:T(128)}, /*index=5*/s32[]{:T(128)}, s32[]{}) while((s32[]{:T(128)}, u32[1024]{0:T(1024)S(1)}, u32[1024]{0:T(1024)S(1)}, s32[1024]{0:T(1024)S(1)}, s32[]{:T(128)}, /*index=5*/s32[]{:T(128)}, s32[]{}) %tuple.130), condition=%wide.region_16.24_spmd.clone, body=%wide.region_15.23_spmd.clone.sunk | while | flops 19460 | bytes 67685 | solution.py:44
  92.7 4.5 gather_fusion.1
  97.3 4.5 gather_fusion.1
  101.9 4.5 gather_fusion.1
  106.5 4.5 gather_fusion.1
  111.1 4.5 gather_fusion.1
  115.7 4.5 gather_fusion.1
  120.3 4.5 gather_fusion.1
  124.9 4.5 gather_fusion.1
  129.6 4.5 gather_fusion.1
  134.2 4.5 gather_fusion.1
  138.8 4.5 gather_fusion.1
  146.8 10.5 %scatter_custom_fusion = f32[257,2048]{0,1:T(8,128)} fusion(s32[1024]{0:T(1024)S(1)} %get-tuple-element.286, f32[]{:T(128)} %constant.182.clone.1, f32[]{:T(128)} %constant.164.clone.2, pred[1024]{0:T(1024)(128)(4,1)S(1)} %get-tuple-element.260, f32[257,1024]{0,1:T(8,128)S(1)} %copy.82, s32[1024]{0:T(1024)S(1)} %fusion.64), kind=kCustom, calls=%fused_computation.30 | custom fusion | flops 263168 | bytes 3683336 | tf_op jit(solution)/shard_map/scatter | solution.py:52
  157.2 13.0 %all-to-all-start = ((f32[257,64,32]{0,2,1:T(8,128)}), f32[257,64,32]{0,2,1:T(8,128)S(1)}, u32[]{:S(2)}, u32[]{:S(2)}) async-start(f32[257,64,32]{0,2,1:T(8,128)} %bitcast.257), calls=%async_computation | async-start | bytes 6291456 | tf_op jit(solution)/shard_map/all_to_all | solution.py:55
  170.5 72.2 %all-to-all-done = f32[257,64,32]{0,2,1:T(8,128)S(1)} async-done(((f32[257,64,32]{0,2,1:T(8,128)}), f32[257,64,32]{0,2,1:T(8,128)S(1)}, u32[]{:S(2)}, u32[]{:S(2)}) %all-to-all-start) | async-done | bytes 2105376 | tf_op jit(solution)/shard_map/all_to_all | solution.py:55
  242.6 2.6 slice_bitcast_fusion.13
  245.2 3.8 copy.83
  249.0 5.1 fusion.13
  255.7 3.1 broadcast_add_fusion.2
  261.6 6.0 fusion.78
  268.2 8.3 all-gather.5.cloned.1.call-done
  279.2 47.3 %custom-call.25 = f32[4,128,128]{2,1,0:T(8,128)S(1)} custom-call(f32[4,128,128]{2,1,0:T(8,128)S(1)} %cholesky.198), custom_call_target="Cholesky" | custom-call | tf_op jit(solution)/shard_map/jit(cholesky)/cholesky | solution.py:66
  326.7 39.3 %custom-call.26 = f32[4,1,128,128]{2,3,1,0:T(8,128)S(1)} custom-call(f32[4,1,128,128]{3,2,1,0:T(8,128)S(1)} %select_bitcast_fusion.1), custom_call_target="InvertDiagBlocksLowerTriangular" | custom-call | tf_op jit(solution)/shard_map/jit(cholesky)/cholesky | solution.py:66
  367.1 46.9 %custom-call.27 = f32[4,128,128]{2,1,0:T(8,128)S(1)} custom-call(f32[4,128,128]{2,1,0:T(8,128)S(1)} %convolution_subtract_fusion.1), custom_call_target="Cholesky" | custom-call | tf_op jit(solution)/shard_map/jit(cholesky)/cholesky | solution.py:66
  414.6 4.2 while.49
  419.4 78.8 %custom-call.29 = f32[4,2,128,128]{2,3,1,0:T(8,128)S(1)} custom-call(f32[4,2,128,128]{3,2,1,0:T(8,128)S(1)} %bitcast.260), custom_call_target="InvertDiagBlocksLowerTriangular" | custom-call | tf_op jit(solution)/shard_map/triangular_solve/custom-call.4 | solution.py:70
  500.9 53.3 %all-gather = f32[256,64,1]{1,2,0:T(1,128)S(1)} all-gather(f32[4,64,1]{1,2,0:T(1,128)S(1)} %fusion.70), channel_id=2, replica_groups=mesh['path'=64,'rep'=4] {'path'}, dimensions={0}, use_global_device_ids=true | all-gather | bytes 66560 | tf_op jit(solution)/shard_map/all_gather | solution.py:74
  554.2 2.8 gather_fusion.4
  557.4 7.2 psum.14
  565.5 10.6 %scatter_custom_fusion.1 = f32[257,2048]{0,1:T(8,128)} fusion(s32[1024]{0:T(1024)} %get-tuple-element.285, f32[]{:T(128)} %constant.182.clone.1, f32[]{:T(128)} %constant.164.clone.2, pred[1024]{0:T(1024)(128)(4,1)S(1)} %copy-done.26, f32[257,1024]{0,1:T(8,128)S(1)} %copy.92, s32[1024]{0:T(1024)S(1)} %copy-done.14), kind=kCustom, calls=%fused_computation.28 | custom fusion | flops 263168 | bytes 3164160 | tf_op jit(solution)/shard_map/scatter | solution.py:52
  576.1 82.5 %all_to_all.10 = f32[257,64,32]{0,2,1:T(8,128)S(1)} all-to-all(f32[257,64,32]{0,2,1:T(8,128)} %bitcast.258), channel_id=1, replica_groups=mesh['path'=64,'rep'=4] {'path'}, dimensions={1} | all-to-all | bytes 4210688 | tf_op jit(solution)/shard_map/all_to_all | solution.py:55
  658.6 2.6 slice_bitcast_fusion.12
  661.2 3.8 copy.93
  665.0 5.1 fusion.16
  672.3 2.8 fusion.12
  676.1 1.8 copy.145
  677.9 5.9 fusion.79
  685.0 4.6 all-gather.7.cloned.1.call-done
  692.3 47.1 %custom-call.30 = f32[4,128,128]{2,1,0:T(8,128)S(1)} custom-call(f32[4,128,128]{2,1,0:T(8,128)S(1)} %cholesky.201), custom_call_target="Cholesky" | custom-call | tf_op jit(solution)/shard_map/jit(cholesky)/cholesky | solution.py:66
  739.6 39.3 %custom-call.31 = f32[4,1,128,128]{2,3,1,0:T(8,128)S(1)} custom-call(f32[4,1,128,128]{3,2,1,0:T(8,128)S(1)} %select_bitcast_fusion), custom_call_target="InvertDiagBlocksLowerTriangular" | custom-call | tf_op jit(solution)/shard_map/jit(cholesky)/cholesky | solution.py:66
  780.0 46.9 %custom-call.32 = f32[4,128,128]{2,1,0:T(8,128)S(1)} custom-call(f32[4,128,128]{2,1,0:T(8,128)S(1)} %convolution_subtract_fusion), custom_call_target="Cholesky" | custom-call | tf_op jit(solution)/shard_map/jit(cholesky)/cholesky | solution.py:66
  827.6 4.0 while.50
  831.6 78.9 %custom-call.34 = f32[4,2,128,128]{2,3,1,0:T(8,128)S(1)} custom-call(f32[4,2,128,128]{3,2,1,0:T(8,128)S(1)} %bitcast.259), custom_call_target="InvertDiagBlocksLowerTriangular" | custom-call | tf_op jit(solution)/shard_map/triangular_solve/custom-call.4 | solution.py:70
  913.2 53.3 %all-gather.1 = f32[256,64,1]{1,2,0:T(1,128)S(1)} all-gather(f32[4,64,1]{1,2,0:T(1,128)S(1)} %fusion.69), channel_id=3, replica_groups=mesh['path'=64,'rep'=4] {'path'}, dimensions={0}, use_global_device_ids=true | all-gather | bytes 66560 | tf_op jit(solution)/shard_map/all_gather | solution.py:74
  966.5 2.8 gather_fusion.7
  969.7 7.2 psum.15
  (264 shorter events, 42.5 us)
Async XLA Ops:
  7.2 137.4 %copy-start = (f32[223,32]{0,1:T(8,128)S(1)}, f32[223,32]{0,1:T(8,128)}, u32[]{:S(2)}) copy-start(f32[223,32]{0,1:T(8,128)} %param.26) | copy-start | bytes 85636
  7.2 0.8 copy-start.1
  86.9 0.6 copy-start.13
  92.6 50.7 %copy-start.9 = (f32[32,1024]{1,0:T(8,128)S(1)}, f32[32,1024]{1,0:T(8,128)}, u32[]{:S(2)}) copy-start(f32[32,1024]{1,0:T(8,128)} %param.23) | copy-start | bytes 393220
  92.6 50.7 %copy-start.11 = (f32[2,32,1024]{2,1,0:T(8,128)S(1)}, f32[2,32,1024]{2,1,0:T(8,128)}, u32[]{:S(2)}) copy-start(f32[2,32,1024]{2,1,0:T(8,128)} %param.24) | copy-start | bytes 786436
  92.7 50.7 %copy-start.12 = (f32[32,32]{1,0:T(8,128)S(1)}, f32[32,32]{1,0:T(8,128)}, u32[]{:S(2)}) copy-start(f32[32,32]{1,0:T(8,128)} %param.25) | copy-start | bytes 12292
  144.3 1.2 copy-start.7
  157.2 85.4 %all-to-all-start = ((f32[257,64,32]{0,2,1:T(8,128)}), f32[257,64,32]{0,2,1:T(8,128)S(1)}, u32[]{:S(2)}, u32[]{:S(2)}) async-start(f32[257,64,32]{0,2,1:T(8,128)} %bitcast.257), calls=%async_computation | async-start | bytes 6291456 | tf_op jit(solution)/shard_map/all_to_all | solution.py:55
  170.2 106.3 %all-gather.5.cloned.1.call-start = ((), (), s32[]{:S(2)}) async-start(), calls=%async_computation.2 | async-start | bytes 1310720 | tf_op jit(solution)/shard_map/all_gather | solution.py:63
  254.2 435.4 %all-gather.7.cloned.1.call-start = ((), (), s32[]{:S(2)}) async-start(), calls=%async_computation.3 | async-start | bytes 1310720 | tf_op jit(solution)/shard_map/all_gather | solution.py:63
  255.1 0.6 copy-start.24
  277.8 1.2 copy-start.2
  367.1 47.4 %copy-start.31 = (s32[2]{0:T(128)S(1)}, s32[2]{0:T(128)}, u32[]{:S(2)}) copy-start(s32[2]{0:T(128)} %iota_multiply_fusion) | copy-start | bytes 28
  414.6 83.6 %copy-start.23 = (f32[4,128,1]{1,0,2:T(4,128)S(1)}, f32[4,128,1]{1,0,2:T(4,128)}, u32[]{:S(2)}) copy-start(f32[4,128,1]{1,0,2:T(4,128)} %slice.172) | copy-start | bytes 6148
  418.8 0.6 copy-start.29
  500.9 53.3 %copy-start.15 = (f32[4,64,1]{1,2,0:T(1,128)}, f32[4,64,1]{1,2,0:T(1,128)S(1)}, u32[]{:S(2)}) copy-start(f32[4,64,1]{1,2,0:T(1,128)S(1)} %fusion.70) | copy-start | bytes 3076
  554.2 3.1 copy-start.5
  554.2 3.1 copy-start.8
  554.2 3.1 copy-start.28
  557.0 7.6 copy-start.17
  557.0 7.6 copy-start.4
  564.8 0.7 copy-start.14
  564.8 0.7 copy-start.26
  665.0 7.3 copy-start.25
  683.8 0.6 copy-start.19
  690.9 1.2 copy-start.3
  826.9 0.7 copy-start.30
  827.4 83.1 %copy-start.22 = (f32[4,128,1]{1,0,2:T(4,128)S(1)}, f32[4,128,1]{1,0,2:T(4,128)}, u32[]{:S(2)}) copy-start(f32[4,128,1]{1,0,2:T(4,128)} %slice.179) | copy-start | bytes 6148
  827.6 83.8 %copy-start.20 = (f32[4,1,256,1]{2,0,1,3:T(4,128)S(1)}, f32[4,1,256,1]{2,0,1,3:T(4,128)}, u32[]{:S(2)}) copy-start(f32[4,1,256,1]{2,0,1,3:T(4,128)} %copy-done.19) | copy-start | bytes 12292
  831.5 134.9 %copy-start.21 = (s32[1024]{0:T(1024)S(1)}, s32[1024]{0:T(1024)}, u32[]{:S(2)}) copy-start(s32[1024]{0:T(1024)} %fusion.68) | copy-start | bytes 12292
  966.4 3.1 copy-start.6
  966.4 3.1 copy-start.10
  966.5 3.1 copy-start.27
  969.3 7.6 copy-start.18
  969.3 8.2 copy-start.16
Sparse Core Ops, SparseCore 0:
  254.3 22.1 all-gather.4
  670.2 19.2 all-gather.6
where the time goes:
time: 994 us; the launch traced here: 985 us
  other arithmetic  466 us (47%)
  blocking collectives  204 us (21%)
  local copies, waits for them, and re-layouts  163 us (16%)
  waiting for transfers between devices  85.1 us (9%)
  matrix products  37.5 us (4%)
  between operations  15.3 us (2%)
  starting transfers between devices  13.3 us (1%)
    another operation x18, other arithmetic, backward_period(): factor = jnp.linalg.cholesky(gram_matrix)  268 us
    another operation x10, other arithmetic, backward_period(): lax.linalg.triangular_solve(factor, halfway, left_side=True, lower=True,...  159 us
    all_gather x2, blocking collectives, backward_period(): weight_table = lax.all_gather(weight_block, 'path', axis=0, tiled=True)  107 us
    gather x22, local copies, waits for them, and re-layouts, backward_period(): group_start = jnp.searchsorted(ordered, ordered, side='left')  99.6 us
    all_to_all x1, blocking collectives, backward_period(): lax.all_to_all(outgoing, 'path', split_axis=1, concat_axis=1, tiled=True)  82.5 us
    all_to_all x1, waiting for transfers between devices, backward_period(): lax.all_to_all(outgoing, 'path', split_axis=1, concat_axis=1, tiled=True)  72.2 us
    scatter x2, other arithmetic, backward_period(): outgoing.at[:, position].set(jnp.take(regress_rows, ranking, axis=1))  21 us
  transfers between devices with their start and end apart: 3, of which 3 were waited for; matrix products, arithmetic and copies ran while one was open for 3% of the time, Pallas kernels for 0%

commit v1 on v0

--- a/solution.py
+++ b/solution.py
@@ -71,7 +71,9 @@
         factor, halfway, left_side=True, lower=True, transpose_a=True
     )[:, :, 0]
     weight_block = lax.dynamic_slice_in_dim(weights, rep_index * column_count, column_count, 1)
-    weight_table = lax.all_gather(weight_block, "path", axis=0, tiled=True)
+    weight_table = jnp.concatenate(
+        lax.all_to_all(jnp.stack([weight_block] * lax.axis_size("path")), "path", 0, 0), axis=0
+    )
     picked = jnp.take(weight_table, slot_of, axis=0)
     moments = moment_features(state_now, quad_dirs, offsets)
     moment_block = lax.dynamic_slice_in_dim(moments, rep_index * column_count, column_count, 0)

time: 994 us -> 934 us (0.940)
  blocking collectives: 204 us -> 94.7 us
  starting transfers between devices: 13.3 us -> 38.8 us
  waiting for transfers between devices: 85.1 us -> 106 us
    all_gather x2 -> x0, blocking collectives: 107 us -> none  [backward_period(): weight_table = lax.all_gather(weight_block, 'path', axis=0, tiled=True)]
    all_to_all x0 -> x2, starting transfers between devices: none -> 25.5 us  [backward_period(): lax.all_to_all(jnp.stack([weight_block] * lax.axis_size('path')), 'path',...]
    all_to_all x0 -> x2, waiting for transfers between devices: none -> 19.5 us  [backward_period(): lax.all_to_all(jnp.stack([weight_block] * lax.axis_size('path')), 'path',...]
    another operation x10 -> x8, other arithmetic: 159 us -> 159 us  [backward_period(): lax.linalg.triangular_solve(factor, halfway, left_side=True, lower=True,...]
  transfers between devices with their start and end apart: 3 -> 5, of which waited for: 3 -> 5; matrix products, arithmetic and copies ran while one was open for 3% -> 3% of each run, Pallas kernels for 0% -> 0%
where the time goes in v1:
time: 934 us; the launch traced here: 926 us
  other arithmetic  467 us (50%)
  local copies, waits for them, and re-layouts  165 us (18%)
  waiting for transfers between devices  106 us (11%)
  blocking collectives  94.7 us (10%)
  starting transfers between devices  38.8 us (4%)
  matrix products  37.7 us (4%)
  between operations  15.1 us (2%)
    another operation x18, other arithmetic, backward_period(): factor = jnp.linalg.cholesky(gram_matrix)  268 us
    another operation x8, other arithmetic, backward_period(): lax.linalg.triangular_solve(factor, halfway, left_side=True, lower=True,...  159 us
    gather x22, local copies, waits for them, and re-layouts, backward_period(): group_start = jnp.searchsorted(ordered, ordered, side='left')  99.6 us
    all_to_all x1, blocking collectives, backward_period(): lax.all_to_all(outgoing, 'path', split_axis=1, concat_axis=1, tiled=True)  80.1 us
    all_to_all x1, waiting for transfers between devices, backward_period(): lax.all_to_all(outgoing, 'path', split_axis=1, concat_axis=1, tiled=True)  72.1 us
    all_to_all x2, starting transfers between devices, backward_period(): lax.all_to_all(jnp.stack([weight_block] * lax.axis_size('path')), 'path',...  25.5 us
    scatter x2, other arithmetic, backward_period(): outgoing.at[:, position].set(jnp.take(regress_rows, ranking, axis=1))  21 us
    all_to_all x2, waiting for transfers between devices, backward_period(): lax.all_to_all(jnp.stack([weight_block] * lax.axis_size('path')), 'path',...  19.5 us
  transfers between devices with their start and end apart: 5, of which 5 were waited for; matrix products, arithmetic and copies ran while one was open for 3% of the time, Pallas kernels for 0%

profile of v1, /device:TPU:1, one launch (start us, length us, event | category | flops | bytes accessed | tf_op | source)
XLA Modules:
  0.0 925.9 jit_solution(8350163669753964044)
XLA Ops:
  7.9 6.9 gather_fusion.2
  15.4 4.4 sort.31
  19.8 4.5 gather_fusion.3
  24.3 50.7 %while.47 = (s32[]{:T(128)}, u32[1024]{0:T(1024)S(1)}, u32[1024]{0:T(1024)S(1)}, s32[1024]{0:T(1024)S(1)}, s32[]{:T(128)}, /*index=5*/s32[]{:T(128)}, s32[]{}) while((s32[]{:T(128)}, u32[1024]{0:T(1024)S(1)}, u32[1024]{0:T(1024)S(1)}, s32[1024]{0:T(1024)S(1)}, s32[]{:T(128)}, /*index=5*/s32[]{:T(128)}, s32[]{}) %tuple.135), condition=%wide.region_3.0_spmd.clone, body=%wide.region_2.5_spmd.clone.sunk | while | flops 19460 | bytes 67685 | solution.py:44
  24.4 4.5 gather_fusion
  29.0 4.5 gather_fusion
  33.6 4.5 gather_fusion
  38.2 4.5 gather_fusion
  42.8 4.5 gather_fusion
  47.4 4.5 gather_fusion
  52.0 4.5 gather_fusion
  56.7 4.5 gather_fusion
  61.3 4.5 gather_fusion
  65.9 4.5 gather_fusion
  70.5 4.5 gather_fusion
  75.1 6.9 gather_fusion.5
  82.6 4.4 sort.32
  87.5 4.5 gather_fusion.6
  92.7 50.7 %while.48 = (s32[]{:T(128)}, u32[1024]{0:T(1024)S(1)}, u32[1024]{0:T(1024)S(1)}, s32[1024]{0:T(1024)S(1)}, s32[]{:T(128)}, /*index=5*/s32[]{:T(128)}, s32[]{}) while((s32[]{:T(128)}, u32[1024]{0:T(1024)S(1)}, u32[1024]{0:T(1024)S(1)}, s32[1024]{0:T(1024)S(1)}, s32[]{:T(128)}, /*index=5*/s32[]{:T(128)}, s32[]{}) %tuple.132), condition=%wide.region_16.24_spmd.clone, body=%wide.region_15.23_spmd.clone.sunk | while | flops 19460 | bytes 67685 | solution.py:44
  92.7 4.5 gather_fusion.1
  97.3 4.5 gather_fusion.1
  101.9 4.5 gather_fusion.1
  106.5 4.5 gather_fusion.1
  111.1 4.5 gather_fusion.1
  115.7 4.5 gather_fusion.1
  120.3 4.5 gather_fusion.1
  124.9 4.5 gather_fusion.1
  129.6 4.5 gather_fusion.1
  134.2 4.5 gather_fusion.1
  138.8 4.5 gather_fusion.1
  146.8 10.5 %scatter_custom_fusion = f32[257,2048]{0,1:T(8,128)} fusion(s32[1024]{0:T(1024)S(1)} %get-tuple-element.290, f32[]{:T(128)} %constant.182.clone.1, f32[]{:T(128)} %constant.164.clone.2, pred[1024]{0:T(1024)(128)(4,1)S(1)} %get-tuple-element.260, f32[257,1024]{0,1:T(8,128)S(1)} %copy.82, s32[1024]{0:T(1024)S(1)} %fusion.68), kind=kCustom, calls=%fused_computation.30 | custom fusion | flops 263168 | bytes 3683336 | tf_op jit(solution)/shard_map/scatter | solution.py:52
  157.2 13.0 %all-to-all-start = ((f32[257,64,32]{0,2,1:T(8,128)}), f32[257,64,32]{0,2,1:T(8,128)S(1)}, u32[]{:S(2)}, u32[]{:S(2)}) async-start(f32[257,64,32]{0,2,1:T(8,128)} %bitcast.259), calls=%async_computation | async-start | bytes 6291456 | tf_op jit(solution)/shard_map/all_to_all | solution.py:55
  170.6 72.1 %all-to-all-done = f32[257,64,32]{0,2,1:T(8,128)S(1)} async-done(((f32[257,64,32]{0,2,1:T(8,128)}), f32[257,64,32]{0,2,1:T(8,128)S(1)}, u32[]{:S(2)}, u32[]{:S(2)}) %all-to-all-start) | async-done | bytes 2105376 | tf_op jit(solution)/shard_map/all_to_all | solution.py:55
  242.6 2.6 fusion.88
  245.2 3.8 copy.83
  249.0 5.1 fusion.13
  255.6 3.1 broadcast_add_fusion.2
  261.6 6.0 fusion.90
  268.1 8.3 all-gather.3.cloned.1.call-done
  279.2 47.4 %custom-call.25 = f32[4,128,128]{2,1,0:T(8,128)S(1)} custom-call(f32[4,128,128]{2,1,0:T(8,128)S(1)} %cholesky.198), custom_call_target="Cholesky" | custom-call | tf_op jit(solution)/shard_map/jit(cholesky)/cholesky | solution.py:66
  326.7 39.3 %custom-call.26 = f32[4,1,128,128]{2,3,1,0:T(8,128)S(1)} custom-call(f32[4,1,128,128]{3,2,1,0:T(8,128)S(1)} %select_bitcast_fusion.1), custom_call_target="InvertDiagBlocksLowerTriangular" | custom-call | tf_op jit(solution)/shard_map/jit(cholesky)/cholesky | solution.py:66
  367.1 46.9 %custom-call.27 = f32[4,128,128]{2,1,0:T(8,128)S(1)} custom-call(f32[4,128,128]{2,1,0:T(8,128)S(1)} %convolution_subtract_fusion.1), custom_call_target="Cholesky" | custom-call | tf_op jit(solution)/shard_map/jit(cholesky)/cholesky | solution.py:66
  414.7 4.2 while.49
  419.5 78.8 %custom-call.29 = f32[4,2,128,128]{2,3,1,0:T(8,128)S(1)} custom-call(f32[4,2,128,128]{3,2,1,0:T(8,128)S(1)} %bitcast.262), custom_call_target="InvertDiagBlocksLowerTriangular" | custom-call | tf_op jit(solution)/shard_map/triangular_solve/custom-call.4 | solution.py:70
  502.3 12.7 %all-to-all-start.1 = ((f32[64,1,256]{2,1,0:T(1,128)}), f32[64,1,256]{2,1,0:T(1,128)S(1)}, u32[]{:S(2)}, u32[]{:S(2)}) async-start(f32[64,1,256]{2,1,0:T(1,128)} %reshape.419), calls=%async_computation.1 | async-start | bytes 131072 | tf_op jit(solution)/shard_map/all_to_all | solution.py:75
  515.1 10.0 %all-to-all-done.1 = f32[64,1,256]{2,1,0:T(1,128)S(1)} async-done(((f32[64,1,256]{2,1,0:T(1,128)}), f32[64,1,256]{2,1,0:T(1,128)S(1)}, u32[]{:S(2)}, u32[]{:S(2)}) %all-to-all-start.1) | async-done | bytes 65568 | tf_op jit(solution)/shard_map/all_to_all | solution.py:75
  526.6 2.8 gather_fusion.4
  529.8 7.3 psum.14
  537.9 10.6 %scatter_custom_fusion.1 = f32[257,2048]{0,1:T(8,128)} fusion(s32[1024]{0:T(1024)} %get-tuple-element.289, f32[]{:T(128)} %constant.182.clone.1, f32[]{:T(128)} %constant.164.clone.2, pred[1024]{0:T(1024)(128)(4,1)S(1)} %copy-done.22, f32[257,1024]{0,1:T(8,128)S(1)} %copy.92, s32[1024]{0:T(1024)S(1)} %copy-done.14), kind=kCustom, calls=%fused_computation.28 | custom fusion | flops 263168 | bytes 3164160 | tf_op jit(solution)/shard_map/scatter | solution.py:52
  548.5 80.1 %all_to_all.20 = f32[257,64,32]{0,2,1:T(8,128)S(1)} all-to-all(f32[257,64,32]{0,2,1:T(8,128)} %bitcast.260), channel_id=1, replica_groups=mesh['path'=64,'rep'=4] {'path'}, dimensions={1} | all-to-all | bytes 4210688 | tf_op jit(solution)/shard_map/all_to_all | solution.py:55
  631.2 3.8 copy.93
  635.0 5.1 fusion.16
  640.8 2.8 fusion.12
  646.4 6.1 fusion.91
  653.1 6.5 all-gather.5.cloned.1.call-done
  662.3 47.3 %custom-call.30 = f32[4,128,128]{2,1,0:T(8,128)S(1)} custom-call(f32[4,128,128]{2,1,0:T(8,128)S(1)} %cholesky.201), custom_call_target="Cholesky" | custom-call | tf_op jit(solution)/shard_map/jit(cholesky)/cholesky | solution.py:66
  709.8 39.3 %custom-call.31 = f32[4,1,128,128]{2,3,1,0:T(8,128)S(1)} custom-call(f32[4,1,128,128]{3,2,1,0:T(8,128)S(1)} %select_bitcast_fusion), custom_call_target="InvertDiagBlocksLowerTriangular" | custom-call | tf_op jit(solution)/shard_map/jit(cholesky)/cholesky | solution.py:66
  750.2 46.9 %custom-call.32 = f32[4,128,128]{2,1,0:T(8,128)S(1)} custom-call(f32[4,128,128]{2,1,0:T(8,128)S(1)} %convolution_subtract_fusion), custom_call_target="Cholesky" | custom-call | tf_op jit(solution)/shard_map/jit(cholesky)/cholesky | solution.py:66
  797.7 4.0 while.50
  801.8 78.8 %custom-call.34 = f32[4,2,128,128]{2,3,1,0:T(8,128)S(1)} custom-call(f32[4,2,128,128]{3,2,1,0:T(8,128)S(1)} %bitcast.261), custom_call_target="InvertDiagBlocksLowerTriangular" | custom-call | tf_op jit(solution)/shard_map/triangular_solve/custom-call.4 | solution.py:70
  884.1 12.7 %all-to-all-start.3 = ((f32[64,1,256]{2,1,0:T(1,128)}), f32[64,1,256]{2,1,0:T(1,128)S(1)}, u32[]{:S(2)}, u32[]{:S(2)}) async-start(f32[64,1,256]{2,1,0:T(1,128)} %reshape.421), calls=%async_computation.3 | async-start | bytes 131072 | tf_op jit(solution)/shard_map/all_to_all | solution.py:75
  897.5 9.4 %all-to-all-done.3 = f32[64,1,256]{2,1,0:T(1,128)S(1)} async-done(((f32[64,1,256]{2,1,0:T(1,128)}), f32[64,1,256]{2,1,0:T(1,128)S(1)}, u32[]{:S(2)}, u32[]{:S(2)}) %all-to-all-start.3) | async-done | bytes 65568 | tf_op jit(solution)/shard_map/all_to_all | solution.py:75
  907.8 2.8 gather_fusion.7
  911.0 7.3 psum.15
  (267 shorter events, 49.3 us)
Async XLA Ops:
  7.2 137.4 %copy-start = (f32[223,32]{0,1:T(8,128)S(1)}, f32[223,32]{0,1:T(8,128)}, u32[]{:S(2)}) copy-start(f32[223,32]{0,1:T(8,128)} %param.26) | copy-start | bytes 85636
  7.2 0.8 copy-start.1
  86.9 0.6 copy-start.13
  92.6 50.7 %copy-start.9 = (f32[32,1024]{1,0:T(8,128)S(1)}, f32[32,1024]{1,0:T(8,128)}, u32[]{:S(2)}) copy-start(f32[32,1024]{1,0:T(8,128)} %param.23) | copy-start | bytes 393220
  92.6 50.7 %copy-start.11 = (f32[2,32,1024]{2,1,0:T(8,128)S(1)}, f32[2,32,1024]{2,1,0:T(8,128)}, u32[]{:S(2)}) copy-start(f32[2,32,1024]{2,1,0:T(8,128)} %param.24) | copy-start | bytes 786436
  92.7 50.7 %copy-start.12 = (f32[32,32]{1,0:T(8,128)S(1)}, f32[32,32]{1,0:T(8,128)}, u32[]{:S(2)}) copy-start(f32[32,32]{1,0:T(8,128)} %param.25) | copy-start | bytes 12292
  144.3 1.2 copy-start.7
  157.2 85.4 %all-to-all-start = ((f32[257,64,32]{0,2,1:T(8,128)}), f32[257,64,32]{0,2,1:T(8,128)S(1)}, u32[]{:S(2)}, u32[]{:S(2)}) async-start(f32[257,64,32]{0,2,1:T(8,128)} %bitcast.259), calls=%async_computation | async-start | bytes 6291456 | tf_op jit(solution)/shard_map/all_to_all | solution.py:55
  170.2 106.2 %all-gather.3.cloned.1.call-start = ((), (), s32[]{:S(2)}) async-start(), calls=%async_computation.4 | async-start | bytes 1310720 | tf_op jit(solution)/shard_map/all_gather | solution.py:63
  255.0 0.6 copy-start.20
  277.8 1.2 copy-start.2
  367.1 47.4 %copy-start.27 = (s32[2]{0:T(128)S(1)}, s32[2]{0:T(128)}, u32[]{:S(2)}) copy-start(s32[2]{0:T(128)} %iota_multiply_fusion) | copy-start | bytes 28
  414.6 83.6 %copy-start.18 = (f32[4,128,1]{1,0,2:T(4,128)S(1)}, f32[4,128,1]{1,0,2:T(4,128)}, u32[]{:S(2)}) copy-start(f32[4,128,1]{1,0,2:T(4,128)} %slice.172) | copy-start | bytes 6148
  418.9 0.6 copy-start.25
  502.3 22.8 %all-to-all-start.1 = ((f32[64,1,256]{2,1,0:T(1,128)}), f32[64,1,256]{2,1,0:T(1,128)S(1)}, u32[]{:S(2)}, u32[]{:S(2)}) async-start(f32[64,1,256]{2,1,0:T(1,128)} %reshape.419), calls=%async_computation.1 | async-start | bytes 131072 | tf_op jit(solution)/shard_map/all_to_all | solution.py:75
  515.0 144.6 %all-gather.5.cloned.1.call-start = ((), (), s32[]{:S(2)}) async-start(), calls=%async_computation.5 | async-start | bytes 1310720 | tf_op jit(solution)/shard_map/all_gather | solution.py:63
  526.6 3.1 copy-start.5
  526.6 3.1 copy-start.8
  526.6 3.1 copy-start.24
  529.4 7.6 copy-start.15
  529.4 7.6 copy-start.4
  537.2 0.7 copy-start.14
  537.3 0.7 copy-start.22
  635.0 5.8 copy-start.21
  660.9 1.2 copy-start.3
  797.1 0.7 copy-start.26
  797.6 83.0 %copy-start.17 = (f32[4,128,1]{1,0,2:T(4,128)S(1)}, f32[4,128,1]{1,0,2:T(4,128)}, u32[]{:S(2)}) copy-start(f32[4,128,1]{1,0,2:T(4,128)} %slice.179) | copy-start | bytes 6148
  801.7 95.1 %copy-start.10 = (f32[32,1024]{1,0:T(8,128)S(1)}, f32[32,1024]{1,0:T(8,128)}, u32[]{:S(2)}) copy-start(f32[32,1024]{1,0:T(8,128)} %param.23) | copy-start | bytes 393220
  801.7 95.1 %copy-start.19 = (f32[1,4,64]{2,1,0:T(4,128)S(1)}, f32[1,4,64]{2,1,0:T(4,128)}, u32[]{:S(2)}) copy-start(f32[1,4,64]{2,1,0:T(4,128)} %get-tuple-element.275) | copy-start | bytes 3076
  801.7 106.0 %copy-start.16 = (s32[1024]{0:T(1024)S(1)}, s32[1024]{0:T(1024)}, u32[]{:S(2)}) copy-start(s32[1024]{0:T(1024)} %fusion.72) | copy-start | bytes 12292
  884.1 22.8 %all-to-all-start.3 = ((f32[64,1,256]{2,1,0:T(1,128)}), f32[64,1,256]{2,1,0:T(1,128)S(1)}, u32[]{:S(2)}, u32[]{:S(2)}) async-start(f32[64,1,256]{2,1,0:T(1,128)} %reshape.421), calls=%async_computation.3 | async-start | bytes 131072 | tf_op jit(solution)/shard_map/all_to_all | solution.py:75
  907.8 3.0 copy-start.6
  907.8 3.0 copy-start.23
Sparse Core Ops, SparseCore 0:
  254.3 22.1 all-gather.2
  640.3 19.2 all-gather.4
